TPU v7x, 32 devices: a whole 2x2x4 slice. The times are simulated.
32 devices in a mesh: row: 4 (over z), col: 8 (over y, x, core).
Axes of the slice: x: 2, y: 2, z: 4, core: 2. Of those that a mesh axis runs over, the one named last changes fastest.
Arguments:
- xn: bfloat16 [256, 2048], P('col', 'row'), may hold values from -6 to 6
- w_qkv: bfloat16 [2048, 6144], P('row', 'col'), may hold values from -0.125 to 0.125
- w_out: bfloat16 [2048, 2048], P('col', 'row'), may hold values from -0.125 to 0.125
- pool: bfloat16 [1024, 64, 4096], P('row', None, 'col'), may hold values from -136 to 136
- page_table: int32 [256, 64], P('row'), may hold values from 0 to 271
- lengths: int32 [256], P('row'), may hold values from 1 to 4096, 24576 in all
- mig_src: int32 [64], replicated, may hold values from 0 to 1023, as said below
- deal: int32 [256], replicated, may hold values from 0 to 255, each once
Outputs:
- attended: bfloat16 [256, 2048], P('col', 'row')
- landed: bfloat16 [64, 64, 4096], P('row', None, 'col')
Inputs may be any that keep to these rules, and one draw needn't show every extreme that they name: `page_table`: page ids of a request refer to its own row block: below 256 its pool pages, from 256 its landing slots. `lengths`: the longest request has exactly 4096 cache tokens. `mig_src`: slot d belongs to row block d // 16; its source page lies in the pool pages of another row block. `deal`: a permutation of the requests.
All inputs are finite; a program needn't handle non-finite values. No bound on the sum of `lengths` on one device may be relied on, other than what follows from the above.
Results may differ from a plain program's by a relative error of at most 0.02.
Values may be sent and summed in bfloat16 or wider, within the bound.
No kernel may reach another device: no remote copies, remote signals or barrier semaphores. Data moves between devices by JAX's collectives and lax.ppermute only.
A program may use at most 128 MiB of HBM per device.

v0:
```python
import functools

import jax
import jax.numpy as jnp
from jax import lax
from jax.experimental import pallas as pl
from jax.experimental.pallas import tpu as pltpu
from jax.sharding import PartitionSpec as P

HEAD_DIM = 64
PAGE = 64


theta_base = 130000.0
neg_large = -1e30


def rotate(values, positions):
    half = values.shape[-1] // 2
    freqs = theta_base ** (-(jnp.arange(half, dtype=jnp.float32) * 2.0 / values.shape[-1]))
    angles = positions.astype(jnp.float32)[:, None, None] * freqs[None, None, :]
    cosine = jnp.cos(angles)
    sine = jnp.sin(angles)
    first = values[..., :half]
    second = values[..., half:]
    return jnp.concatenate(
        [first * cosine - second * sine, second * cosine + first * sine], axis=-1
    )


def page_scores(page_of, flat, scores, qrow, start, count, length, maxp):
    rows = qrow.shape[0]
    pos = lax.broadcasted_iota(jnp.int32, (rows, PAGE), 1)

    def one(k):
        j = flat[start + k] % maxp
        s = lax.dot_general(
            qrow, page_of(start + k), (((1,), (1,)), ((), ())),
            preferred_element_type=jnp.float32,
        ) * 0.125
        s = jnp.where(j * PAGE + pos < length, s, neg_large)
        scores[k] = s
        return s

    def two(k2, top):
        s0 = one(2 * k2)
        s1 = one(2 * k2 + 1)
        return jnp.maximum(top, jnp.maximum(s0, s1))

    top = lax.fori_loop(0, count // 2, two, jnp.full((rows, PAGE), neg_large, jnp.float32))
    top = lax.fori_loop(count // 2 * 2, count, lambda k, t: jnp.maximum(t, one(k)), top)
    return jnp.max(top, axis=1, keepdims=True)


def page_values(page_of, flat, scores, top, start, count, length, maxp, lanes):
    rows = top.shape[0]
    pos = lax.broadcasted_iota(jnp.int32, (rows, PAGE), 1)

    def one(k):
        j = flat[start + k] % maxp
        e = jnp.where(j * PAGE + pos < length, jnp.exp(scores[k] - top), 0.0)
        w = e.astype(jnp.bfloat16)
        return e, jnp.dot(w, page_of(start + k), preferred_element_type=jnp.float32)

    def two(k2, carry):
        total, numer = carry
        e0, n0 = one(2 * k2)
        e1, n1 = one(2 * k2 + 1)
        return total + (e0 + e1), numer + (n0 + n1)

    def single(k, carry):
        total, numer = carry
        e0, n0 = one(k)
        return total + e0, numer + n0

    init = (jnp.zeros((rows, PAGE), jnp.float32), jnp.zeros((rows, lanes), jnp.float32))
    carry = lax.fori_loop(0, count // 2, two, init)
    total, numer = lax.fori_loop(count // 2 * 2, count, single, carry)
    return jnp.sum(total, axis=1, keepdims=True), numer


def build_list(tbl, lens, pool_n, maxp, reqs, flat, starts, listed, landing):
    def req(r, carry):
        n, nl = carry
        starts[r] = n
        count = (lens[r] + PAGE - 1) // PAGE

        def page(j, n):
            e = r * maxp + j
            flat[n] = e
            keep = (tbl[e] >= pool_n) if landing else (tbl[e] < pool_n)
            return n + keep.astype(jnp.int32)

        n2 = lax.fori_loop(0, count, page, n)
        listed[nl] = r
        return n2, nl + (n2 > n).astype(jnp.int32)

    n, nl = lax.fori_loop(0, reqs, req, (0, 0))
    starts[reqs] = n
    return n, nl


def pool_kernel(tbl, lens, qrow_ref, snew_ref, pool_ref,
                m_ref, l_ref, n_ref, scores, flat, starts, listed):
    reqs, rows, lanes = qrow_ref.shape
    maxp = scores.shape[0]
    pool_n = pool_ref.shape[0]
    build_list(tbl, lens, pool_n, maxp, reqs, flat, starts, listed, False)
    page_of = lambda f: pool_ref[jnp.clip(tbl[flat[f]], 0, pool_n - 1)]

    def request(r, carry):
        start = starts[r]
        count = starts[r + 1] - start
        length = lens[r]
        snew = snew_ref[r][:, :1]
        top = page_scores(page_of, flat, scores, qrow_ref[r], start, count, length, maxp)
        top = jnp.maximum(top, snew)
        total, numer = page_values(page_of, flat, scores, top, start, count, length, maxp,
                                   lanes)
        m_ref[r] = jnp.broadcast_to(top, (rows, 128))
        l_ref[r] = jnp.broadcast_to(total, (rows, 128))
        n_ref[r] = numer
        return carry

    lax.fori_loop(0, reqs, request, 0)


def land_kernel(tbl, lens, qrow_ref, m_in, l_in, n_in, land_ref, pool_n_ref,
                m_ref, l_ref, n_ref, scores, flat, starts, listed):
    reqs, rows, lanes = qrow_ref.shape
    maxp = scores.shape[0]
    pool_n = pool_n_ref.shape[0]
    land_n = land_ref.shape[0]
    _, listed_n = build_list(tbl, lens, pool_n, maxp, reqs, flat, starts, listed, True)
    m_ref[...] = m_in[...]
    l_ref[...] = l_in[...]
    n_ref[...] = n_in[...]
    page_of = lambda f: land_ref[jnp.clip(tbl[flat[f]] - pool_n, 0, land_n - 1)]

    def request(k, carry):
        r = listed[k]
        start = starts[r]
        count = starts[r + 1] - start
        length = lens[r]
        top_a = m_in[r][:, :1]
        top_b = page_scores(page_of, flat, scores, qrow_ref[r], start, count, length, maxp)
        top = jnp.maximum(top_a, top_b)
        total, numer = page_values(page_of, flat, scores, top, start, count, length, maxp,
                                   lanes)
        scale = jnp.exp(top_a - top)
        m_ref[r] = jnp.broadcast_to(top, (rows, 128))
        l_ref[r] = jnp.broadcast_to(total + l_in[r][:, :1] * scale, (rows, 128))
        n_ref[r] = numer + n_in[r] * scale
        return carry

    lax.fori_loop(0, listed_n, request, 0)


def attend(query, key_new, value_new, table, lens, pool, landed_fn):
    req_count, heads_here, _ = query.shape
    lanes = pool.shape[2]
    maxp = table.shape[1]
    pool_n = pool.shape[0]
    rows = 8
    qf = query.astype(jnp.float32)
    score_new = jnp.sum(qf * key_new.astype(jnp.float32), axis=-1) * 0.125
    eye = jnp.eye(rows, heads_here, dtype=jnp.float32)
    zeros = jnp.zeros_like(qf)
    qrow = (eye[None, :, :, None, None] *
            jnp.stack([qf, zeros], axis=2)[:, None, :, :, :]).reshape(req_count, rows, lanes)
    qrow = qrow.astype(jnp.bfloat16)
    vf = value_new.astype(jnp.float32)
    snew = jnp.zeros((req_count, rows, 128), jnp.float32) + jnp.pad(
        score_new, ((0, 0), (0, rows - heads_here)))[:, :, None]
    tbl = table.reshape(-1)

    full = lambda shape: pl.BlockSpec(shape, lambda i, *_: (0,) * len(shape))
    big = (req_count, rows, lanes)
    small = (req_count, rows, 128)
    scratch = [
        pltpu.VMEM((maxp, rows, PAGE), jnp.float32),
        pltpu.SMEM((req_count * maxp,), jnp.int32),
        pltpu.SMEM((req_count + 1,), jnp.int32),
        pltpu.SMEM((req_count,), jnp.int32),
    ]
    params = pltpu.CompilerParams(
        dimension_semantics=("arbitrary",), vmem_limit_bytes=60 * 1024 * 1024)
    state = [
        jax.ShapeDtypeStruct(small, jnp.float32),
        jax.ShapeDtypeStruct(small, jnp.float32),
        jax.ShapeDtypeStruct(big, jnp.float32),
    ]
    m_a, l_a, n_a = pl.pallas_call(
        pool_kernel,
        grid_spec=pltpu.PrefetchScalarGridSpec(
            num_scalar_prefetch=2,
            grid=(1,),
            in_specs=[full(big), full(small), pl.BlockSpec(memory_space=pltpu.VMEM)],
            out_specs=[full(small), full(small), full(big)],
            scratch_shapes=scratch,
        ),
        out_shape=state,
        compiler_params=params,
    )(tbl, lens, qrow, snew, pool)

    landed = landed_fn(n_a)
    m_b, l_b, n_b = pl.pallas_call(
        land_kernel,
        grid_spec=pltpu.PrefetchScalarGridSpec(
            num_scalar_prefetch=2,
            grid=(1,),
            in_specs=[full(big), full(small), full(small), full(big),
                      pl.BlockSpec(memory_space=pltpu.VMEM), pl.BlockSpec(memory_space=pl.ANY)],
            out_specs=[full(small), full(small), full(big)],
            scratch_shapes=scratch,
        ),
        out_shape=state,
        compiler_params=params,
    )(tbl, lens, qrow, m_a, l_a, n_a, landed, pool)
    top = m_b[:, :heads_here, :1]
    e_new = jnp.exp(score_new[:, :, None] - top)
    w_new = e_new.astype(jnp.bfloat16).astype(jnp.float32)
    numer = n_b[:, :heads_here].reshape(req_count, heads_here, heads_here, 2, HEAD_DIM)
    numer = jnp.stack([numer[:, h, h, 1] for h in range(heads_here)], axis=1)
    picked = ((numer + w_new * vf) / (l_b[:, :heads_here, :1] + e_new)).astype(jnp.bfloat16)
    return picked, landed


def migration_plan(pool, mig_src, row_count):
    pool_dev = pool.shape[0]
    land_all = mig_src.shape[0]
    land_dev = land_all // row_count
    src_row = jnp.clip(mig_src // pool_dev, 0, row_count - 1)
    local_page = jnp.clip(mig_src - src_row * pool_dev, 0, pool_dev - 1)
    dst_row = jnp.arange(land_all, dtype=jnp.int32) // land_dev
    onehot = (src_row[:, None] == jnp.arange(row_count, dtype=jnp.int32)[None, :]).astype(jnp.int32)
    csum = jnp.cumsum(onehot.reshape(row_count, land_dev, row_count), axis=1)
    csum = csum.reshape(land_all, row_count)
    rank = jnp.sum(csum * onehot, axis=1) - 1
    return dict(src_row=src_row, local_page=local_page, dst_row=dst_row, rank=rank,
                most=jnp.max(csum), land_dev=land_dev, first=max(1, (land_dev * 5 + 7) // 8))


def outgoing_pages(pool, plan, row_count, lo, size):
    my_row = lax.axis_index("row")
    rank = plan["rank"]
    sel = (plan["src_row"] == my_row) & (rank >= lo) & (rank < lo + size)
    where = jnp.where(sel, plan["dst_row"] * size + (rank - lo), row_count * size)
    idx = jnp.zeros((row_count * size,), jnp.int32).at[where].set(plan["local_page"], mode="drop")
    return jnp.take(pool, idx, axis=0).reshape(row_count, size, pool.shape[1], pool.shape[2])


def migrate_first(pool, mig_src, row_count):
    plan = migration_plan(pool, mig_src, row_count)
    sent = outgoing_pages(pool, plan, row_count, 0, plan["first"])
    return lax.all_to_all(sent, "row", split_axis=0, concat_axis=0, tiled=True)


def migrate_rest(pool, mig_src, row_count, first_recv, dep):
    plan = migration_plan(pool, mig_src, row_count)
    land_dev, k1 = plan["land_dev"], plan["first"]
    my_row = lax.axis_index("row")
    mine = my_row * land_dev + jnp.arange(land_dev, dtype=jnp.int32)
    src_mine = plan["src_row"][mine]
    rank_mine = plan["rank"][mine]
    pool_dep, _ = lax.optimization_barrier((pool, dep))
    sizes = [0, land_dev - k1] if land_dev > k1 else [0]

    def branch(size):
        def run(pool_b, recv1):
            if size == 0:
                both = recv1
            else:
                sent = outgoing_pages(pool_b, plan, row_count, k1, size)
                recv2 = lax.all_to_all(sent, "row", split_axis=0, concat_axis=0, tiled=True)
                both = jnp.concatenate([recv1, recv2], axis=1)
            width = k1 + size
            flat = both.reshape(row_count * width, both.shape[2], both.shape[3])
            return jnp.take(flat, src_mine * width + jnp.clip(rank_mine, 0, width - 1), axis=0)
        return run

    need = jnp.maximum(plan["most"] - k1, 0)
    index = jnp.sum((jnp.array(sizes, jnp.int32) < need).astype(jnp.int32))
    return lax.switch(index, [branch(b) for b in sizes], pool_dep, first_recv)


def on_device(xn, w_qkv, w_out, pool, page_table, lengths, mig_src, deal):
    heads_here = w_out.shape[0] // HEAD_DIM
    rows_all = xn.shape[0] * lax.axis_size("col")
    row_count = lax.axis_size("row")
    req_row = rows_all // row_count
    inverse = jnp.zeros((rows_all,), jnp.int32).at[deal].set(jnp.arange(rows_all, dtype=jnp.int32))
    gathered = lax.all_gather(xn, "col", axis=0, tiled=True)
    chosen = inverse
    partial = jnp.dot(jnp.take(gathered, chosen, axis=0), w_qkv,
                      preferred_element_type=jnp.float32).astype(jnp.bfloat16)
    parts = lax.all_to_all(partial, "row", split_axis=0, concat_axis=0, tiled=True)
    projected = jnp.sum(parts.reshape(row_count, req_row, -1).astype(jnp.float32), axis=0)
    projected = projected.reshape(req_row, heads_here, 3, HEAD_DIM)
    query = rotate(projected[:, :, 0], lengths).astype(jnp.bfloat16)
    key_new = rotate(projected[:, :, 1], lengths).astype(jnp.bfloat16)
    value_new = projected[:, :, 2].astype(jnp.bfloat16)
    first = migrate_first(pool, mig_src, row_count)
    mixed, landed = attend(query, key_new, value_new, page_table, lengths, pool,
                           lambda dep: migrate_rest(pool, mig_src, row_count, first, dep))
    mixed = mixed.reshape(req_row, heads_here * HEAD_DIM)
    mixed_all = lax.all_gather(mixed, "row", axis=0, tiled=True)
    chosen = deal
    col_count = lax.axis_size("col")
    partial = jnp.dot(
        jnp.take(mixed_all, chosen, axis=0), w_out, preferred_element_type=jnp.float32
    ).astype(jnp.bfloat16)
    parts = lax.all_to_all(partial, "col", split_axis=0, concat_axis=0, tiled=True)
    attended = jnp.sum(
        parts.reshape(col_count, rows_all // col_count, -1).astype(jnp.float32), axis=0
    ).astype(jnp.bfloat16)
    return (attended, landed)


def solution(mesh):
    placed = (
        P("col", "row"),
        P("row", "col"),
        P("col", "row"),
        P("row", None, "col"),
        P("row", None),
        P("row"),
        P(),
        P(),
    )
    return jax.shard_map(
        on_device,
        mesh=mesh,
        in_specs=placed,
        out_specs=(P("col", "row"), P("row", None, "col")),
        check_vma=False,
    )
```

profile of v0, /device:TPU:0, one launch (start us, length us, event | category | flops | bytes accessed | tf_op | source)
XLA Modules:
  0.0 157.9 jit_solution(15142845513248009044)
XLA Ops:
  0.7 0.8 compare_select_fusion.5
  1.4 1.4 scatter_custom_fusion.1
  2.9 11.0 %all_gather.6 = bf16[256,512]{1,0:T(8,128)(2,1)S(1)} all-gather(bf16[32,512]{1,0:T(8,128)(2,1)} %param.11), channel_id=1, replica_groups=mesh['row'=4,'col'=8] {'col'}, dimensions={0}, use_global_device_ids=true | all-gather | bytes 294912 | tf_op jit(solution)/shard_map/all_gather | solution.py:293
  13.8 1.2 gather_fusion.3
  15.0 1.2 convolution_convert_fusion
  16.2 4.9 %all-to-all-start.1 = ((bf16[4,64,768]{2,1,0:T(8,128)(2,1)}), bf16[4,64,768]{2,1,0:T(8,128)(2,1)}, u32[]{:S(2)}, u32[]{:S(2)}) async-start(bf16[4,64,768]{2,1,0:T(8,128)(2,1)} %bitcast.3), calls=%async_computation.1 | async-start | bytes 786432 | tf_op jit(solution)/shard_map/all_to_all | solution.py:297
  21.3 0.8 select_reduce_fusion
  22.1 0.8 scatter_custom_fusion.2
  23.0 6.5 %gather_fusion.6 = bf16[40,64,512]{2,1,0:T(8,128)(2,1)S(1)} fusion(bf16[256,64,512]{2,1,0:T(8,128)(2,1)} %pool_n_ref.1, s32[1024]{0:T(1024)S(1)} %pad_clamp_fusion.4), kind=kCustom, calls=%fused_computation.6 | custom fusion | bytes 5243040 | tf_op jit(solution)/shard_map/jit(_take)/gather | solution.py:250
  29.5 1.8 %broadcast_select_fusion.3 = bf16[4,10,64,512]{3,2,1,0:T(8,128)(2,1)} fusion(bf16[4,10,64,512]{3,2,1,0:T(8,128)(2,1)S(1)} %bitcast.33, pred[4,10]{1,0:T(4,128)(4,1)S(1)} %broadcast_in_dim.115), kind=kLoop, calls=%fused_computation.28 | loop fusion | flops 1310720 | bytes 5242920 | tf_op jit(solution)/shard_map/jit(_take)/select_n | solution.py:250
  31.4 2.0 %all-to-all-done.1 = bf16[4,64,768]{2,1,0:T(8,128)(2,1)} async-done(((bf16[4,64,768]{2,1,0:T(8,128)(2,1)}), bf16[4,64,768]{2,1,0:T(8,128)(2,1)}, u32[]{:S(2)}, u32[]{:S(2)}) %all-to-all-start.1) | async-done | bytes 393248 | tf_op jit(solution)/shard_map/all_to_all | solution.py:297
  33.3 3.7 %all-to-all-start.2 = ((bf16[4,10,64,512]{3,2,1,0:T(8,128)(2,1)}), bf16[4,10,64,512]{3,2,1,0:T(8,128)(2,1)S(1)}, u32[]{:S(2)}, u32[]{:S(2)}) async-start(bf16[4,10,64,512]{3,2,1,0:T(8,128)(2,1)} %broadcast_select_fusion.3), calls=%async_computation.2 | async-start | bytes 5242880 | tf_op jit(solution)/shard_map/all_to_all | solution.py:256
  37.0 1.2 gather_fusion.5
  38.2 1.2 gather_fusion.4
  39.5 0.7 mul.164
  40.2 0.7 reshape.230.tbl
  41.5 0.6 fusion.16
  42.8 0.5 and_select_fusion.1
  43.4 0.6 compare_and_fusion.5
  44.0 0.8 multiply_cosine_fusion
  44.8 1.7 %convert_reduce_fusion = f32[64,768]{1,0:T(8,128)} fusion(bf16[4,64,768]{2,1,0:T(8,128)(2,1)} %all-to-all-done.1), kind=kLoop, calls=%fused_computation.32 | loop fusion | flops 344064 | bytes 589824 | tf_op jit(solution)/shard_map/reduce_sum | solution.py:298
  46.5 2.0 %reshape.231 = f32[64,4,3,64]{3,2,1,0:T(4,128)} reshape(f32[64,768]{1,0:T(8,128)} %convert_reduce_fusion) | data formatting | bytes 393216 | tf_op jit(solution)/shard_map/reshape | solution.py:299
  48.5 3.0 %fusion.9 = (f32[64,4,64]{2,1,0:T(4,128)}, f32[64,4,1,64]{3,2,1,0:T(1,128)S(1)}, f32[64,4,1,64]{3,2,1,0:T(1,128)S(1)}) fusion(f32[64,4,3,64]{3,2,1,0:T(4,128)} %reshape.231), kind=kLoop, calls=%fused_computation.42 | loop fusion | flops 16384 | bytes 360448 | tf_op jit(solution)/shard_map/convert_element_type | solution.py:172
  51.5 0.9 subtract_convert_fusion
  52.5 0.2 multiply_reduce_fusion
  52.7 0.7 copy.68
  53.5 0.9 copy.53
  54.4 1.2 reshape.233
  55.6 1.4 fusion.25
  57.0 1.6 %multiply_convert_fusion.qrow_ref = bf16[64,8,512]{2,1,0:T(8,128)(2,1)} fusion(f32[64,512]{1,0:T(8,128)S(1)} %reshape.233, f32[8,512]{1,0:T(8,128)} %mul.164), kind=kLoop, calls=%fused_computation.31 | loop fusion | flops 524288 | bytes 671744 | tf_op jit(solution)/shard_map/convert_element_type | solution.py:171
  58.6 0.8 add.112.snew_ref
  59.4 54.2 %shard_map.104 = (f32[64,8,128]{2,1,0:T(8,128)}, f32[64,8,128]{2,1,0:T(8,128)}, f32[64,8,512]{2,1,0:T(8,128)}) custom-call(s32[4096]{0:T(1024)} %reshape.230.tbl, s32[64]{0:T(128)} %lens.3, bf16[64,8,512]{2,1,0:T(8,128)(2,1)} %multiply_convert_fusion.qrow_ref, f32[64,8,128]{2,1,0:T(8,128)} %add.112.snew_ref, bf16[256,64,512]{2,1,0:T(8,128)(2,1)} %pool_n_ref.1), custom_call_target="tpu_custom_call" | custom-call | tf_op jit(solution)/shard_map/pallas_call | solution.py:193
  113.6 1.3 copy.61
  114.8 1.7 %reshape.235 = f32[64,256]{1,0:T(8,128)} reshape(f32[64,4,64]{2,1,0:T(4,128)} %get-tuple-element.64) | data formatting | bytes 131072 | tf_op jit(solution)/shard_map/convert_element_type | solution.py:172
  116.5 3.6 %conditional.1 = (bf16[16,64,512]{2,1,0:T(8,128)(2,1)S(1)}) conditional(s32[]{:T(128)} %clamp.7, (s32[16]{0:T(128)}, s32[16]{0:T(128)S(1)}, bf16[4,10,64,512]{3,2,1,0:T(8,128)(2,1)S(1)}) %tuple.38, (s32[16]{0:T(128)}, s32[16]{0:T(128)S(1)}, s32[64]{0:T(128)S(1)}, s32[64]{0:T(128)S(1)}, s32[64]{0:T(128)}, /*index=5*/s32[64]{0:T(128)}, ...), branch_computations={%region_8.9_spmd, %region_9.11_spmd} | conditional | flops 3411051 | bytes 23604164 | solution.py:284
  116.5 0.6 compare_and_fusion
  117.1 1.6 %gather_fusion = bf16[16,64,512]{2,1,0:T(8,128)(2,1)} fusion(bf16[40,64,512]{2,1,0:T(8,128)(2,1)S(1)} %bitcast.32, s32[1024]{0:T(1024)S(1)} %pad_clamp_fusion), kind=kCustom, calls=%fused_computation | custom fusion | bytes 2097216 | tf_op jit(solution)/shard_map/cond/branch_0_fun/jit(_take)/gather | solution.py:279
  118.7 1.4 broadcast_select_fusion
  120.1 9.1 %shard_map.105 = (f32[64,8,128]{2,1,0:T(8,128)}, f32[64,8,128]{2,1,0:T(8,128)}, f32[64,8,512]{2,1,0:T(8,128)}) custom-call(s32[4096]{0:T(1024)} %reshape.230.tbl, s32[64]{0:T(128)} %lens.3, bf16[64,8,512]{2,1,0:T(8,128)(2,1)} %multiply_convert_fusion.qrow_ref, f32[64,8,128]{2,1,0:T(8,128)} %get-tuple-element.45.m_in, f32[64,8,128]{2,1,0:T(8,128)} %get-tuple-element.46.l_in, ...), custom_call_target="tpu_custom_call" | custom-call | tf_op jit(solution)/shard_map/pallas_call | solution.py:207
  129.2 1.4 slice.49
  130.6 0.8 reshape.232
  132.2 0.1 div.53
  132.6 0.1 mul.193
  132.9 13.4 %all_gather.7 = bf16[256,256]{1,0:T(8,128)(2,1)S(1)} all-gather(bf16[64,256]{1,0:T(8,128)(2,1)S(1)} %divide_convert_fusion), channel_id=1, replica_groups=mesh['row'=4,'col'=8] {'row'}, dimensions={0}, use_global_device_ids=true | all-gather | bytes 163840 | tf_op jit(solution)/shard_map/all_gather | solution.py:307
  146.3 1.2 gather_fusion.7
  147.5 0.3 convolution_convert_fusion.1
  147.8 9.5 %all_to_all.27 = bf16[8,32,512]{2,1,0:T(8,128)(2,1)S(1)} all-to-all(bf16[8,32,512]{2,1,0:T(8,128)(2,1)S(1)} %bitcast.36), channel_id=1, replica_groups=mesh['row'=4,'col'=8] {'col'}, dimensions={0} | all-to-all | bytes 524288 | tf_op jit(solution)/shard_map/all_to_all | solution.py:313
  157.2 0.7 reduce_sum.56
  (65 shorter events, 1.9 us)
Async XLA Ops:
  0.6 14.4 %copy-start = (bf16[512,768]{1,0:T(8,128)(2,1)S(1)}, bf16[512,768]{1,0:T(8,128)(2,1)}, u32[]{:S(2)}) copy-start(bf16[512,768]{1,0:T(8,128)(2,1)} %param.12) | copy-start | bytes 2359300
  0.6 20.4 %copy-start.13 = (s32[64]{0:T(128)S(1)}, s32[64]{0:T(128)}, u32[]{:S(2)}) copy-start(s32[64]{0:T(128)} %param.17) | copy-start | bytes 772
  16.2 17.2 %all-to-all-start.1 = ((bf16[4,64,768]{2,1,0:T(8,128)(2,1)}), bf16[4,64,768]{2,1,0:T(8,128)(2,1)}, u32[]{:S(2)}, u32[]{:S(2)}) async-start(bf16[4,64,768]{2,1,0:T(8,128)(2,1)} %bitcast.3), calls=%async_computation.1 | async-start | bytes 786432 | tf_op jit(solution)/shard_map/all_to_all | solution.py:297
  21.0 1.9 %copy-start.14 = (s32[64]{0:T(128)}, s32[64]{0:T(128)S(1)}, u32[]{:S(2)}) copy-start(s32[64]{0:T(128)S(1)} %get-tuple-element.58) | copy-start | bytes 772
  31.4 8.1 %copy-start.9 = (s32[64]{0:T(128)S(1)}, s32[64]{0:T(128)}, u32[]{:S(2)}) copy-start(s32[64]{0:T(128)} %lens.3) | copy-start | bytes 772
  31.4 8.9 %copy-start.6 = (s32[64,64]{1,0:T(8,128)S(1)}, s32[64,64]{1,0:T(8,128)}, u32[]{:S(2)}) copy-start(s32[64,64]{1,0:T(8,128)} %param.15) | copy-start | bytes 49156
  31.4 12.0 %copy-start.11 = (s32[256]{0:T(256)S(1)}, s32[256]{0:T(256)}, u32[]{:S(2)}) copy-start(s32[256]{0:T(256)} %param.18) | copy-start | bytes 3076
  33.3 83.2 %all-to-all-start.2 = ((bf16[4,10,64,512]{3,2,1,0:T(8,128)(2,1)}), bf16[4,10,64,512]{3,2,1,0:T(8,128)(2,1)S(1)}, u32[]{:S(2)}, u32[]{:S(2)}) async-start(bf16[4,10,64,512]{3,2,1,0:T(8,128)(2,1)} %broadcast_select_fusion.3), calls=%async_computation.2 | async-start | bytes 5242880 | tf_op jit(solution)/shard_map/all_to_all | solution.py:256
  59.4 57.1 %copy-start.7 = (s32[16]{0:T(128)S(1)}, s32[16]{0:T(128)}, u32[]{:S(2)}) copy-start(s32[16]{0:T(128)} %gather_fusion.5) | copy-start | bytes 196
  120.1 9.1 %copy-start.1 = (bf16[16,64,512]{2,1,0:T(8,128)(2,1)}, bf16[16,64,512]{2,1,0:T(8,128)(2,1)S(1)}, u32[]{:S(2)}) copy-start(bf16[16,64,512]{2,1,0:T(8,128)(2,1)S(1)} %get-tuple-element.81.land_ref) | copy-start | bytes 3145732
  129.2 2.6 %copy-start.4 = (f32[64,8,128]{2,1,0:T(8,128)S(1)}, f32[64,8,128]{2,1,0:T(8,128)}, u32[]{:S(2)}) copy-start(f32[64,8,128]{2,1,0:T(8,128)} %get-tuple-element.50) | copy-start | bytes 786436
  129.2 2.6 %copy-start.5 = (f32[64,8,128]{2,1,0:T(8,128)S(1)}, f32[64,8,128]{2,1,0:T(8,128)}, u32[]{:S(2)}) copy-start(f32[64,8,128]{2,1,0:T(8,128)} %get-tuple-element.51) | copy-start | bytes 786436
  129.2 3.7 %copy-start.3 = (f32[64,256]{1,0:T(8,128)S(1)}, f32[64,256]{1,0:T(8,128)}, u32[]{:S(2)}) copy-start(f32[64,256]{1,0:T(8,128)} %reshape.235) | copy-start | bytes 196612
  130.6 16.9 %copy-start.2 = (bf16[256,512]{1,0:T(8,128)(2,1)S(1)}, bf16[256,512]{1,0:T(8,128)(2,1)}, u32[]{:S(2)}) copy-start(bf16[256,512]{1,0:T(8,128)(2,1)} %param.13) | copy-start | bytes 786436
  130.6 16.9 %copy-start.12 = (pred[256]{0:T(512)(128)(4,1)S(1)}, pred[256]{0:T(512)(128)(4,1)}, u32[]{:S(2)}) copy-start(pred[256]{0:T(512)(128)(4,1)} %compare_and_fusion.5) | copy-start | bytes 772
where the time goes:
time: 159 us; the launch traced here: 158 us
  Pallas kernels  63.2 us (40%)
  blocking collectives  33.8 us (21%)
  local copies, waits for them, and re-layouts  28.8 us (18%)
  other arithmetic  17.8 us (11%)
  starting transfers between devices  8.52 us (5%)
  between operations  2.25 us (1%)
  waiting for transfers between devices  1.97 us (1%)
    pallas_call x1, Pallas kernels, attend(): pl.pallas_call(pool_kernel, grid_spec=pltpu.PrefetchScalarGridSpec(num_sc...  54.2 us
    all_gather x1, blocking collectives, on_device(): mixed_all = lax.all_gather(mixed, 'row', axis=0, tiled=True)  13.4 us
    all_gather x1, blocking collectives, on_device(): gathered = lax.all_gather(xn, 'col', axis=0, tiled=True)  11 us
    all_to_all x1, blocking collectives, on_device(): lax.all_to_all(partial, 'col', split_axis=0, concat_axis=0, tiled=True)  9.47 us
    pallas_call x1, Pallas kernels, attend(): pl.pallas_call(land_kernel, grid_spec=pltpu.PrefetchScalarGridSpec(num_sc...  9.07 us
    gather x1, local copies, waits for them, and re-layouts, outgoing_pages(): jnp.take(pool, idx, axis=0)  6.49 us
    all_to_all x1, starting transfers between devices, on_device(): lax.all_to_all(partial, 'row', split_axis=0, concat_axis=0, tiled=True)  4.87 us
    all_to_all x1, starting transfers between devices, migrate_first(): return lax.all_to_all(sent, 'row', split_axis=0, concat_axis=0, tiled=True)  3.65 us
  transfers between devices with their start and end apart: 2, of which 1 were waited for; matrix products, arithmetic and copies ran while one was open for 22% of the time, Pallas kernels for 34%

commit v1 on v0

--- a/solution.py
+++ b/solution.py
@@ -100,9 +100,17 @@
     return n, nl
 
 
+def query_rows(qwide_ref, r, rows):
+    lanes = qwide_ref.shape[2]
+    wide = jnp.broadcast_to(qwide_ref[r], (rows, lanes))
+    head = lax.broadcasted_iota(jnp.int32, (rows, lanes), 0)
+    lane = lax.broadcasted_iota(jnp.int32, (rows, lanes), 1)
+    return jnp.where(head == lane // 128, wide, 0.0).astype(jnp.bfloat16)
+
+
 def pool_kernel(tbl, lens, qrow_ref, snew_ref, pool_ref,
                 m_ref, l_ref, n_ref, scores, flat, starts, listed):
-    reqs, rows, lanes = qrow_ref.shape
+    reqs, rows, lanes = snew_ref.shape[0], snew_ref.shape[1], pool_ref.shape[2]
     maxp = scores.shape[0]
     pool_n = pool_ref.shape[0]
     build_list(tbl, lens, pool_n, maxp, reqs, flat, starts, listed, False)
@@ -113,7 +121,8 @@
         count = starts[r + 1] - start
         length = lens[r]
         snew = snew_ref[r][:, :1]
-        top = page_scores(page_of, flat, scores, qrow_ref[r], start, count, length, maxp)
+        top = page_scores(page_of, flat, scores, query_rows(qrow_ref, r, rows), start, count,
+                          length, maxp)
         top = jnp.maximum(top, snew)
         total, numer = page_values(page_of, flat, scores, top, start, count, length, maxp,
                                    lanes)
@@ -127,7 +136,7 @@
 
 def land_kernel(tbl, lens, qrow_ref, m_in, l_in, n_in, land_ref, pool_n_ref,
                 m_ref, l_ref, n_ref, scores, flat, starts, listed):
-    reqs, rows, lanes = qrow_ref.shape
+    reqs, rows, lanes = m_in.shape[0], m_in.shape[1], land_ref.shape[2]
     maxp = scores.shape[0]
     pool_n = pool_n_ref.shape[0]
     land_n = land_ref.shape[0]
@@ -143,7 +152,8 @@
         count = starts[r + 1] - start
         length = lens[r]
         top_a = m_in[r][:, :1]
-        top_b = page_scores(page_of, flat, scores, qrow_ref[r], start, count, length, maxp)
+        top_b = page_scores(page_of, flat, scores, query_rows(qrow_ref, r, rows), start, count,
+                            length, maxp)
         top = jnp.maximum(top_a, top_b)
         total, numer = page_values(page_of, flat, scores, top, start, count, length, maxp,
                                    lanes)
@@ -156,20 +166,19 @@
     lax.fori_loop(0, listed_n, request, 0)
 
 
-def attend(query, key_new, value_new, table, lens, pool, landed_fn):
-    req_count, heads_here, _ = query.shape
+def attend(qk, value_new, table, lens, pool, landed_fn):
+    req_count = qk.shape[0]
     lanes = pool.shape[2]
+    heads_here = lanes // (2 * HEAD_DIM)
     maxp = table.shape[1]
     pool_n = pool.shape[0]
     rows = 8
-    qf = query.astype(jnp.float32)
-    score_new = jnp.sum(qf * key_new.astype(jnp.float32), axis=-1) * 0.125
-    eye = jnp.eye(rows, heads_here, dtype=jnp.float32)
-    zeros = jnp.zeros_like(qf)
-    qrow = (eye[None, :, :, None, None] *
-            jnp.stack([qf, zeros], axis=2)[:, None, :, :, :]).reshape(req_count, rows, lanes)
-    qrow = qrow.astype(jnp.bfloat16)
-    vf = value_new.astype(jnp.float32)
+    lane = jnp.arange(lanes, dtype=jnp.int32)
+    qwide = jnp.where((lane % 128 < HEAD_DIM)[None, :], qk.astype(jnp.float32), 0.0)
+    qwide = qwide.reshape(req_count, 1, lanes)
+    grouped = qk.astype(jnp.float32).reshape(req_count, heads_here, 2 * HEAD_DIM)
+    score_new = jnp.sum(grouped[..., :HEAD_DIM] * grouped[..., HEAD_DIM:], axis=-1) * 0.125
+    vf = value_new.astype(jnp.float32).reshape(req_count, heads_here, HEAD_DIM)
     snew = jnp.zeros((req_count, rows, 128), jnp.float32) + jnp.pad(
         score_new, ((0, 0), (0, rows - heads_here)))[:, :, None]
     tbl = table.reshape(-1)
@@ -177,6 +186,7 @@
     full = lambda shape: pl.BlockSpec(shape, lambda i, *_: (0,) * len(shape))
     big = (req_count, rows, lanes)
     small = (req_count, rows, 128)
+    wide = (req_count, 1, lanes)
     scratch = [
         pltpu.VMEM((maxp, rows, PAGE), jnp.float32),
         pltpu.SMEM((req_count * maxp,), jnp.int32),
@@ -195,13 +205,13 @@
         grid_spec=pltpu.PrefetchScalarGridSpec(
             num_scalar_prefetch=2,
             grid=(1,),
-            in_specs=[full(big), full(small), pl.BlockSpec(memory_space=pltpu.VMEM)],
+            in_specs=[full(wide), full(small), pl.BlockSpec(memory_space=pltpu.VMEM)],
             out_specs=[full(small), full(small), full(big)],
             scratch_shapes=scratch,
         ),
         out_shape=state,
         compiler_params=params,
-    )(tbl, lens, qrow, snew, pool)
+    )(tbl, lens, qwide, snew, pool)
 
     landed = landed_fn(n_a)
     m_b, l_b, n_b = pl.pallas_call(
@@ -209,14 +219,14 @@
         grid_spec=pltpu.PrefetchScalarGridSpec(
             num_scalar_prefetch=2,
             grid=(1,),
-            in_specs=[full(big), full(small), full(small), full(big),
+            in_specs=[full(wide), full(small), full(small), full(big),
                       pl.BlockSpec(memory_space=pltpu.VMEM), pl.BlockSpec(memory_space=pl.ANY)],
             out_specs=[full(small), full(small), full(big)],
             scratch_shapes=scratch,
         ),
         out_shape=state,
         compiler_params=params,
-    )(tbl, lens, qrow, m_a, l_a, n_a, landed, pool)
+    )(tbl, lens, qwide, m_a, l_a, n_a, landed, pool)
     top = m_b[:, :heads_here, :1]
     e_new = jnp.exp(score_new[:, :, None] - top)
     w_new = e_new.astype(jnp.bfloat16).astype(jnp.float32)
@@ -292,16 +302,31 @@
     inverse = jnp.zeros((rows_all,), jnp.int32).at[deal].set(jnp.arange(rows_all, dtype=jnp.int32))
     gathered = lax.all_gather(xn, "col", axis=0, tiled=True)
     chosen = inverse
-    partial = jnp.dot(jnp.take(gathered, chosen, axis=0), w_qkv,
+    heads3 = w_qkv.reshape(w_qkv.shape[0], heads_here, 3, HEAD_DIM)
+    w_perm = jnp.concatenate(
+        [heads3[:, :, :2].reshape(w_qkv.shape[0], -1), heads3[:, :, 2].reshape(w_qkv.shape[0], -1)],
+        axis=1)
+    partial = jnp.dot(jnp.take(gathered, chosen, axis=0), w_perm,
                       preferred_element_type=jnp.float32).astype(jnp.bfloat16)
     parts = lax.all_to_all(partial, "row", split_axis=0, concat_axis=0, tiled=True)
     projected = jnp.sum(parts.reshape(row_count, req_row, -1).astype(jnp.float32), axis=0)
-    projected = projected.reshape(req_row, heads_here, 3, HEAD_DIM)
-    query = rotate(projected[:, :, 0], lengths).astype(jnp.bfloat16)
-    key_new = rotate(projected[:, :, 1], lengths).astype(jnp.bfloat16)
-    value_new = projected[:, :, 2].astype(jnp.bfloat16)
+    qk_lanes = heads_here * 2 * HEAD_DIM
+    x = projected[:, :qk_lanes]
+    lane = jnp.arange(qk_lanes, dtype=jnp.int32)
+    within = lane % HEAD_DIM
+    half = HEAD_DIM // 2
+    freqs = theta_base ** (-(jnp.arange(half, dtype=jnp.float32) * 2.0 / HEAD_DIM))
+    angles = lengths.astype(jnp.float32)[:, None] * freqs[within % half][None, :]
+    cosine = jnp.cos(angles)
+    sine = jnp.sin(angles)
+    ahead = jnp.roll(x, -half, axis=1)
+    behind = jnp.roll(x, half, axis=1)
+    rotated = jnp.where((within < half)[None, :], x * cosine - ahead * sine,
+                        x * cosine + behind * sine)
+    qk = rotated.astype(jnp.bfloat16)
+    value_new = projected[:, qk_lanes:].astype(jnp.bfloat16)
     first = migrate_first(pool, mig_src, row_count)
-    mixed, landed = attend(query, key_new, value_new, page_table, lengths, pool,
+    mixed, landed = attend(qk, value_new, page_table, lengths, pool,
                            lambda dep: migrate_rest(pool, mig_src, row_count, first, dep))
     mixed = mixed.reshape(req_row, heads_here * HEAD_DIM)
     mixed_all = lax.all_gather(mixed, "row", axis=0, tiled=True)

time: 159 us -> 165 us (1.038); the launches traced: 158 us -> 169 us
  blocking collectives: 33.8 us -> 52.4 us
  Pallas kernels: 63.2 us -> 50.5 us
  other arithmetic: 17.8 us -> 28.2 us
  local copies, waits for them, and re-layouts: 28.8 us -> 23.4 us
    gather x0 -> x27, other arithmetic: none -> 20.9 us  [on_device(): freqs[within % half][None, :]]
    all_gather x1, blocking collectives: 13.4 us -> 32.2 us  [on_device(): mixed_all = lax.all_gather(mixed, 'row', axis=0, tiled=True)]
    pallas_call x1, Pallas kernels: 54.2 us -> 42.4 us  [attend(): pl.pallas_call(pool_kernel, grid_spec=pltpu.PrefetchScalarGridSpec(num_sc...]
    convert_element_type x4 -> x1, other arithmetic: 4.59 us -> 0.01 us  [on_device(): lengths.astype(jnp.float32)[:, None] * freqs[within % half][None, :]]
    mul x5 -> x1, local copies, waits for them, and re-layouts: 4.16 us -> 0.5 us  [attend(): jnp.sum(grouped[..., :HEAD_DIM] * grouped[..., HEAD_DIM:], axis=-1) * 0.125]
    reduce_sum x1, other arithmetic: 1.75 us -> 0.06 us  [on_device(): jnp.sum(parts.reshape(row_count, req_row, -1).astype(jnp.float32), axis=0)]
    convert_element_type x1 -> x0, local copies, waits for them, and re-layouts: 1.65 us -> none  [attend(): vf = value_new.astype(jnp.float32)]
  transfers between devices with their start and end apart: 2 -> 2, of which waited for: 1 -> 1; matrix products, arithmetic and copies ran while one was open for 22% -> 23% of each run, Pallas kernels for 34% -> 25%
where the time goes in v1:
time: 165 us; the launch traced here: 169 us
  blocking collectives  52.4 us (32%)
  Pallas kernels  50.5 us (31%)
  other arithmetic  28.2 us (17%)
  local copies, waits for them, and re-layouts  23.4 us (14%)
  starting transfers between devices  8.52 us (5%)
  between operations  2.27 us (1%)
  waiting for transfers between devices  1.89 us (1%)
    pallas_call x1, Pallas kernels, attend(): pl.pallas_call(pool_kernel, grid_spec=pltpu.PrefetchScalarGridSpec(num_sc...  42.4 us
    all_gather x1, blocking collectives, on_device(): mixed_all = lax.all_gather(mixed, 'row', axis=0, tiled=True)  32.2 us
    gather x27, other arithmetic, on_device(): freqs[within % half][None, :]  20.9 us
    all_gather x1, blocking collectives, on_device(): gathered = lax.all_gather(xn, 'col', axis=0, tiled=True)  10.8 us
    all_to_all x1, blocking collectives, on_device(): lax.all_to_all(partial, 'col', split_axis=0, concat_axis=0, tiled=True)  9.5 us
    pallas_call x1, Pallas kernels, attend(): pl.pallas_call(land_kernel, grid_spec=pltpu.PrefetchScalarGridSpec(num_sc...  8.19 us
    gather x1, local copies, waits for them, and re-layouts, outgoing_pages(): jnp.take(pool, idx, axis=0)  6.49 us
    all_to_all x1, starting transfers between devices, on_device(): lax.all_to_all(partial, 'row', split_axis=0, concat_axis=0, tiled=True)  4.87 us
  transfers between devices with their start and end apart: 2, of which 1 were waited for; matrix products, arithmetic and copies ran while one was open for 23% of the time, Pallas kernels for 25%

profile of v1, /device:TPU:0, one launch (start us, length us, event | category | flops | bytes accessed | tf_op | source)
XLA Modules:
  0.0 168.8 jit_solution(9874960949480568944)
XLA Ops:
  0.7 0.7 compare_select_fusion.14
  1.4 1.4 scatter_custom_fusion.1
  2.8 1.4 copy.37
  4.3 10.8 %all_gather.6 = bf16[256,512]{1,0:T(8,128)(2,1)S(1)} all-gather(bf16[32,512]{1,0:T(8,128)(2,1)S(1)} %copy-done.4), channel_id=1, replica_groups=mesh['row'=4,'col'=8] {'col'}, dimensions={0}, use_global_device_ids=true | all-gather | bytes 294912 | tf_op jit(solution)/shard_map/all_gather | solution.py:303
  15.1 1.2 gather_fusion.3
  16.2 1.2 convolution_convert_fusion
  17.4 4.9 %all-to-all-start.1 = ((bf16[4,64,768]{2,1,0:T(8,128)(2,1)}), bf16[4,64,768]{2,1,0:T(8,128)(2,1)S(1)}, u32[]{:S(2)}, u32[]{:S(2)}) async-start(bf16[4,64,768]{2,1,0:T(8,128)(2,1)} %bitcast.6), calls=%async_computation.1 | async-start | bytes 786432 | tf_op jit(solution)/shard_map/all_to_all | solution.py:311
  22.5 0.8 select_reduce_fusion
  23.4 0.8 scatter_custom_fusion.2
  24.3 6.5 %gather_fusion.6 = bf16[40,64,512]{2,1,0:T(8,128)(2,1)S(1)} fusion(bf16[256,64,512]{2,1,0:T(8,128)(2,1)} %pool_n_ref.1, s32[1024]{0:T(1024)S(1)} %pad_clamp_fusion.4), kind=kCustom, calls=%fused_computation.6 | custom fusion | bytes 5243040 | tf_op jit(solution)/shard_map/jit(_take)/gather | solution.py:260
  30.8 1.8 %broadcast_select_fusion.3 = bf16[4,10,64,512]{3,2,1,0:T(8,128)(2,1)} fusion(bf16[4,10,64,512]{3,2,1,0:T(8,128)(2,1)S(1)} %bitcast.66, pred[4,10]{1,0:T(4,128)(4,1)S(1)} %broadcast_in_dim.137), kind=kLoop, calls=%fused_computation.28 | loop fusion | flops 1310720 | bytes 5242920 | tf_op jit(solution)/shard_map/jit(_take)/select_n | solution.py:260
  32.6 1.9 %all-to-all-done.1 = bf16[4,64,768]{2,1,0:T(8,128)(2,1)S(1)} async-done(((bf16[4,64,768]{2,1,0:T(8,128)(2,1)}), bf16[4,64,768]{2,1,0:T(8,128)(2,1)S(1)}, u32[]{:S(2)}, u32[]{:S(2)}) %all-to-all-start.1) | async-done | bytes 393248 | tf_op jit(solution)/shard_map/all_to_all | solution.py:311
  34.5 3.7 %all-to-all-start.2 = ((bf16[4,10,64,512]{3,2,1,0:T(8,128)(2,1)}), bf16[4,10,64,512]{3,2,1,0:T(8,128)(2,1)S(1)}, u32[]{:S(2)}, u32[]{:S(2)}) async-start(bf16[4,10,64,512]{3,2,1,0:T(8,128)(2,1)} %broadcast_select_fusion.3), calls=%async_computation.2 | async-start | bytes 5242880 | tf_op jit(solution)/shard_map/all_to_all | solution.py:266
  38.2 0.7 gather_fusion.5
  38.8 0.7 gather_fusion.4
  39.5 0.7 reshape.214.tbl
  40.8 0.6 fusion.30
  43.0 0.7 fusion.46
  43.7 4.5 %compare_select_fusion.7 = f32[512,1]{0,1:T(1,128)S(1)} fusion(f32[]{:T(128)} %bitcast.32, f32[]{:T(128)} %bitcast.33, f32[]{:T(128)} %bitcast.34, f32[]{:T(128)} %bitcast.35, f32[]{:T(128)} %bitcast.36, f32[]{:T(128)} %bitcast.38, f32[]{:T(128)} %bitcast.37), kind=kLoop, calls=%fused_computation.96 | loop fusion | flops 16384 | bytes 2076 | tf_op jit(solution)/shard_map/gather | solution.py:319
  48.2 0.7 fusion.45
  49.0 15.6 %select_select_fusion = f32[512]{0:T(512)S(1)} fusion(pred[512]{0:T(512)(128)(4,1)S(1)} %compare_reduce_fusion, pred[512]{0:T(512)(128)(4,1)S(1)} %compare_reduce_fusion.1, pred[512]{0:T(512)(128)(4,1)S(1)} %compare_reduce_fusion.2, pred[512]{0:T(512)(128)(4,1)S(1)} %compare_reduce_fusion.3, pred[512]{0:T(512)(128)(4,1)S(1)} %compare_reduce_fusion.4, ...), kind=kLoop, calls=%fused_computation.118 | loop fusion | flops 12800 | bytes 16996 | tf_op jit(solution)/shard_map/gather | solution.py:319
  64.8 0.6 broadcast_select_fusion.4
  65.4 0.7 reshape.217.qrow_ref
  66.1 0.2 fusion.14
  66.4 0.8 add.159.snew_ref
  67.2 42.4 %shard_map.104 = (f32[64,8,128]{2,1,0:T(8,128)}, f32[64,8,128]{2,1,0:T(8,128)}, f32[64,8,512]{2,1,0:T(8,128)}) custom-call(s32[4096]{0:T(1024)} %reshape.214.tbl, s32[64]{0:T(128)} %lens.3, f32[64,1,512]{2,1,0:T(1,128)} %reshape.217.qrow_ref, f32[64,8,128]{2,1,0:T(8,128)} %add.159.snew_ref, bf16[256,64,512]{2,1,0:T(8,128)(2,1)} %pool_n_ref.1), custom_call_target="tpu_custom_call" | custom-call | tf_op jit(solution)/shard_map/pallas_call | solution.py:203
  109.6 0.5 copy.43
  110.1 3.0 %conditional.1 = (bf16[16,64,512]{2,1,0:T(8,128)(2,1)S(1)}) conditional(s32[]{:T(128)} %clamp.7, (s32[16]{0:T(128)S(1)}, s32[16]{0:T(128)S(1)}, bf16[4,10,64,512]{3,2,1,0:T(8,128)(2,1)S(1)}) %tuple.15, (s32[16]{0:T(128)S(1)}, s32[16]{0:T(128)S(1)}, s32[64]{0:T(128)S(1)}, s32[64]{0:T(128)S(1)}, s32[64]{0:T(128)S(1)}, /*index=5*/s32[64]{0:T(128)S(1)}, ...), branch_computations={%region_8.9_spmd, %region_9.11_spmd} | conditional | flops 3411051 | bytes 23603280 | solution.py:294
  110.1 1.6 gather_fusion
  111.7 1.4 broadcast_select_fusion
  113.1 8.2 %shard_map.105 = (f32[64,8,128]{2,1,0:T(8,128)}, f32[64,8,128]{2,1,0:T(8,128)}, f32[64,8,512]{2,1,0:T(8,128)}) custom-call(s32[4096]{0:T(1024)} %reshape.214.tbl, s32[64]{0:T(128)} %lens.3, f32[64,1,512]{2,1,0:T(1,128)} %reshape.217.qrow_ref, f32[64,8,128]{2,1,0:T(8,128)} %get-tuple-element.45.m_in, f32[64,8,128]{2,1,0:T(8,128)} %get-tuple-element.46.l_in, ...), custom_call_target="tpu_custom_call" | custom-call | tf_op jit(solution)/shard_map/pallas_call | solution.py:217
  121.3 1.4 slice.69
  122.7 0.8 reshape.219
  123.5 0.1 slice_bitcast_fusion.3
  123.6 0.2 pad_maximum_fusion.1
  123.8 0.1 stack.6
  124.0 0.1 copy.46
  124.1 0.1 copy.47
  124.2 0.1 div.52
  124.4 0.1 div.53
  124.6 0.1 copy.45
  124.7 0.1 mul.99
  124.8 0.1 mul.100
  125.0 32.2 %all_gather.7 = bf16[256,256]{1,0:T(8,128)(2,1)S(1)} all-gather(bf16[64,256]{1,0:T(8,128)(2,1)S(1)} %divide_convert_fusion), channel_id=1, replica_groups=mesh['row'=4,'col'=8] {'row'}, dimensions={0}, use_global_device_ids=true | all-gather | bytes 163840 | tf_op jit(solution)/shard_map/all_gather | solution.py:332
  157.2 1.2 gather_fusion.7
  158.3 0.3 convolution_convert_fusion.1
  158.6 9.5 %all_to_all.27 = bf16[8,32,512]{2,1,0:T(8,128)(2,1)S(1)} all-to-all(bf16[8,32,512]{2,1,0:T(8,128)(2,1)S(1)} %bitcast.71), channel_id=1, replica_groups=mesh['row'=4,'col'=8] {'col'}, dimensions={0} | all-to-all | bytes 524288 | tf_op jit(solution)/shard_map/all_to_all | solution.py:338
  168.1 0.7 reduce_sum.56
  (80 shorter events, 1.9 us)
Async XLA Ops:
  0.6 157.7 %copy-start = (bf16[256,512]{1,0:T(8,128)(2,1)S(1)}, bf16[256,512]{1,0:T(8,128)(2,1)}, u32[]{:S(2)}) copy-start(bf16[256,512]{1,0:T(8,128)(2,1)} %param.13) | copy-start | bytes 786436
  0.6 3.7 %copy-start.4 = (bf16[32,512]{1,0:T(8,128)(2,1)S(1)}, bf16[32,512]{1,0:T(8,128)(2,1)}, u32[]{:S(2)}) copy-start(bf16[32,512]{1,0:T(8,128)(2,1)} %param.11) | copy-start | bytes 98308
  15.1 7.2 %copy-start.8 = (s32[64]{0:T(128)S(1)}, s32[64]{0:T(128)}, u32[]{:S(2)}) copy-start(s32[64]{0:T(128)} %param.17) | copy-start | bytes 772
  17.4 17.1 %all-to-all-start.1 = ((bf16[4,64,768]{2,1,0:T(8,128)(2,1)}), bf16[4,64,768]{2,1,0:T(8,128)(2,1)S(1)}, u32[]{:S(2)}, u32[]{:S(2)}) async-start(bf16[4,64,768]{2,1,0:T(8,128)(2,1)} %bitcast.6), calls=%async_computation.1 | async-start | bytes 786432 | tf_op jit(solution)/shard_map/all_to_all | solution.py:311
  32.6 6.9 %copy-start.6 = (s32[64]{0:T(128)S(1)}, s32[64]{0:T(128)}, u32[]{:S(2)}) copy-start(s32[64]{0:T(128)} %lens.3) | copy-start | bytes 772
  32.6 6.9 %copy-start.5 = (s32[64,64]{1,0:T(8,128)S(1)}, s32[64,64]{1,0:T(8,128)}, u32[]{:S(2)}) copy-start(s32[64,64]{1,0:T(8,128)} %param.15) | copy-start | bytes 49156
  32.6 16.4 %copy-start.7 = (s32[256]{0:T(256)S(1)}, s32[256]{0:T(256)}, u32[]{:S(2)}) copy-start(s32[256]{0:T(256)} %param.18) | copy-start | bytes 3076
  34.5 75.6 %all-to-all-start.2 = ((bf16[4,10,64,512]{3,2,1,0:T(8,128)(2,1)}), bf16[4,10,64,512]{3,2,1,0:T(8,128)(2,1)S(1)}, u32[]{:S(2)}, u32[]{:S(2)}) async-start(bf16[4,10,64,512]{3,2,1,0:T(8,128)(2,1)} %broadcast_select_fusion.3), calls=%async_computation.2 | async-start | bytes 5242880 | tf_op jit(solution)/shard_map/all_to_all | solution.py:266
  113.1 8.2 %copy-start.1 = (bf16[16,64,512]{2,1,0:T(8,128)(2,1)}, bf16[16,64,512]{2,1,0:T(8,128)(2,1)S(1)}, u32[]{:S(2)}) copy-start(bf16[16,64,512]{2,1,0:T(8,128)(2,1)S(1)} %get-tuple-element.108.land_ref) | copy-start | bytes 3145732
  121.3 2.6 %copy-start.2 = (f32[64,8,128]{2,1,0:T(8,128)S(1)}, f32[64,8,128]{2,1,0:T(8,128)}, u32[]{:S(2)}) copy-start(f32[64,8,128]{2,1,0:T(8,128)} %get-tuple-element.50) | copy-start | bytes 786436
  121.3 2.6 %copy-start.3 = (f32[64,8,128]{2,1,0:T(8,128)S(1)}, f32[64,8,128]{2,1,0:T(8,128)}, u32[]{:S(2)}) copy-start(f32[64,8,128]{2,1,0:T(8,128)} %get-tuple-element.51) | copy-start | bytes 786436

commit v2 on v1

--- a/solution.py
+++ b/solution.py
@@ -108,9 +108,36 @@
     return jnp.where(head == lane // 128, wide, 0.0).astype(jnp.bfloat16)
 
 
-def pool_kernel(tbl, lens, qrow_ref, snew_ref, pool_ref,
-                m_ref, l_ref, n_ref, scores, flat, starts, listed):
-    reqs, rows, lanes = snew_ref.shape[0], snew_ref.shape[1], pool_ref.shape[2]
+def pool_kernel(tbl, lens, x_ref, cos_ref, sin_ref, pool_ref,
+                m_ref, l_ref, n_ref, qrow_ref, snew_ref, scores, flat, starts, listed):
+    reqs, rows, lanes = m_ref.shape[0], m_ref.shape[1], pool_ref.shape[2]
+    half = HEAD_DIM // 2
+    lane = lax.broadcasted_iota(jnp.int32, (1, lanes), 1)
+    first_half = lane % HEAD_DIM < half
+    head = lax.broadcasted_iota(jnp.int32, (rows, lanes), 0)
+    lane8 = lax.broadcasted_iota(jnp.int32, (rows, lanes), 1)
+    own_q = (head == lane8 // 128) & (lane8 % 128 < HEAD_DIM)
+
+    def rotate_row(r):
+        x = x_ref[r]
+        ahead = pltpu.roll(x, lanes - half, 1)
+        behind = pltpu.roll(x, half, 1)
+        c = cos_ref[r]
+        s = sin_ref[r]
+        rot = jnp.where(first_half, x * c - ahead * s, x * c + behind * s)
+        qk = rot.astype(jnp.bfloat16).astype(jnp.float32)
+        keys = pltpu.roll(qk, lanes - HEAD_DIM, 1)
+        prod = jnp.where(own_q, jnp.broadcast_to(qk * keys, (rows, lanes)), 0.0)
+        snew = jnp.sum(prod, axis=1, keepdims=True) * 0.125
+        qrow_ref[r] = jnp.where(lane % 128 < HEAD_DIM, qk, 0.0)
+        snew_ref[r] = jnp.broadcast_to(snew, (rows, 128))
+        return snew
+
+    def prep(r, carry):
+        rotate_row(r)
+        return carry
+
+    lax.fori_loop(0, reqs, prep, 0)
     maxp = scores.shape[0]
     pool_n = pool_ref.shape[0]
     build_list(tbl, lens, pool_n, maxp, reqs, flat, starts, listed, False)
@@ -166,21 +193,21 @@
     lax.fori_loop(0, listed_n, request, 0)
 
 
-def attend(qk, value_new, table, lens, pool, landed_fn):
-    req_count = qk.shape[0]
+def attend(xqk, value_new, table, lens, pool, landed_fn):
+    req_count = xqk.shape[0]
     lanes = pool.shape[2]
     heads_here = lanes // (2 * HEAD_DIM)
     maxp = table.shape[1]
     pool_n = pool.shape[0]
     rows = 8
     lane = jnp.arange(lanes, dtype=jnp.int32)
-    qwide = jnp.where((lane % 128 < HEAD_DIM)[None, :], qk.astype(jnp.float32), 0.0)
-    qwide = qwide.reshape(req_count, 1, lanes)
-    grouped = qk.astype(jnp.float32).reshape(req_count, heads_here, 2 * HEAD_DIM)
-    score_new = jnp.sum(grouped[..., :HEAD_DIM] * grouped[..., HEAD_DIM:], axis=-1) * 0.125
+    half = HEAD_DIM // 2
+    freqs = theta_base ** (-(jnp.arange(half, dtype=jnp.float32) * 2.0 / HEAD_DIM))
+    angles = lens.astype(jnp.float32)[:, None] * freqs[lane % HEAD_DIM % half][None, :]
+    cosine = jnp.cos(angles).reshape(req_count, 1, lanes)
+    sine = jnp.sin(angles).reshape(req_count, 1, lanes)
+    xqk = xqk.reshape(req_count, 1, lanes)
     vf = value_new.astype(jnp.float32).reshape(req_count, heads_here, HEAD_DIM)
-    snew = jnp.zeros((req_count, rows, 128), jnp.float32) + jnp.pad(
-        score_new, ((0, 0), (0, rows - heads_here)))[:, :, None]
     tbl = table.reshape(-1)
 
     full = lambda shape: pl.BlockSpec(shape, lambda i, *_: (0,) * len(shape))
@@ -200,18 +227,20 @@
         jax.ShapeDtypeStruct(small, jnp.float32),
         jax.ShapeDtypeStruct(big, jnp.float32),
     ]
-    m_a, l_a, n_a = pl.pallas_call(
+    m_a, l_a, n_a, qwide, snew = pl.pallas_call(
         pool_kernel,
         grid_spec=pltpu.PrefetchScalarGridSpec(
             num_scalar_prefetch=2,
             grid=(1,),
-            in_specs=[full(wide), full(small), pl.BlockSpec(memory_space=pltpu.VMEM)],
-            out_specs=[full(small), full(small), full(big)],
+            in_specs=[full(wide), full(wide), full(wide), pl.BlockSpec(memory_space=pltpu.VMEM)],
+            out_specs=[full(small), full(small), full(big), full(wide), full(small)],
             scratch_shapes=scratch,
         ),
-        out_shape=state,
+        out_shape=state + [jax.ShapeDtypeStruct(wide, jnp.float32),
+                           jax.ShapeDtypeStruct(small, jnp.float32)],
         compiler_params=params,
-    )(tbl, lens, qwide, snew, pool)
+    )(tbl, lens, xqk, cosine, sine, pool)
+    score_new = snew[:, :heads_here, 0]
 
     landed = landed_fn(n_a)
     m_b, l_b, n_b = pl.pallas_call(
@@ -311,22 +340,9 @@
     parts = lax.all_to_all(partial, "row", split_axis=0, concat_axis=0, tiled=True)
     projected = jnp.sum(parts.reshape(row_count, req_row, -1).astype(jnp.float32), axis=0)
     qk_lanes = heads_here * 2 * HEAD_DIM
-    x = projected[:, :qk_lanes]
-    lane = jnp.arange(qk_lanes, dtype=jnp.int32)
-    within = lane % HEAD_DIM
-    half = HEAD_DIM // 2
-    freqs = theta_base ** (-(jnp.arange(half, dtype=jnp.float32) * 2.0 / HEAD_DIM))
-    angles = lengths.astype(jnp.float32)[:, None] * freqs[within % half][None, :]
-    cosine = jnp.cos(angles)
-    sine = jnp.sin(angles)
-    ahead = jnp.roll(x, -half, axis=1)
-    behind = jnp.roll(x, half, axis=1)
-    rotated = jnp.where((within < half)[None, :], x * cosine - ahead * sine,
-                        x * cosine + behind * sine)
-    qk = rotated.astype(jnp.bfloat16)
     value_new = projected[:, qk_lanes:].astype(jnp.bfloat16)
     first = migrate_first(pool, mig_src, row_count)
-    mixed, landed = attend(qk, value_new, page_table, lengths, pool,
+    mixed, landed = attend(projected[:, :qk_lanes], value_new, page_table, lengths, pool,
                            lambda dep: migrate_rest(pool, mig_src, row_count, first, dep))
     mixed = mixed.reshape(req_row, heads_here * HEAD_DIM)
     mixed_all = lax.all_gather(mixed, "row", axis=0, tiled=True)

time: 165 us -> 190 us (1.15); the launches traced: 169 us -> 189 us
  Pallas kernels: 50.5 us -> 86.9 us
  blocking collectives: 52.4 us -> 33.7 us
  other arithmetic: 28.2 us -> 32.4 us
    pallas_call x1, Pallas kernels: 42.4 us -> 76.1 us  [attend(): pl.pallas_call(pool_kernel, grid_spec=pltpu.PrefetchScalarGridSpec(num_sc...]
    all_gather x1, blocking collectives: 32.2 us -> 13.4 us  [on_device(): mixed_all = lax.all_gather(mixed, 'row', axis=0, tiled=True)]
    sin x0 -> x1, other arithmetic: none -> 5.16 us  [attend(): sine = jnp.sin(angles).reshape(req_count, 1, lanes)]
    pallas_call x1, Pallas kernels: 8.19 us -> 10.8 us  [attend(): pl.pallas_call(land_kernel, grid_spec=pltpu.PrefetchScalarGridSpec(num_sc...]
  transfers between devices with their start and end apart: 2 -> 2, of which waited for: 1 -> 1; matrix products, arithmetic and copies ran while one was open for 23% -> 22% of each run, Pallas kernels for 25% -> 40%
where the time goes in v2:
time: 190 us; the launch traced here: 189 us
  Pallas kernels  86.9 us (46%)
  blocking collectives  33.7 us (18%)
  other arithmetic  32.4 us (17%)
  local copies, waits for them, and re-layouts  22 us (12%)
  starting transfers between devices  8.52 us (4%)
  between operations  2.25 us (1%)
    pallas_call x1, Pallas kernels, attend(): pl.pallas_call(pool_kernel, grid_spec=pltpu.PrefetchScalarGridSpec(num_sc...  76.1 us
    gather x27, other arithmetic, attend(): freqs[lane % HEAD_DIM % half][None, :]  20.9 us
    all_gather x1, blocking collectives, on_device(): mixed_all = lax.all_gather(mixed, 'row', axis=0, tiled=True)  13.4 us
    pallas_call x1, Pallas kernels, attend(): pl.pallas_call(land_kernel, grid_spec=pltpu.PrefetchScalarGridSpec(num_sc...  10.8 us
    all_gather x1, blocking collectives, on_device(): gathered = lax.all_gather(xn, 'col', axis=0, tiled=True)  10.8 us
    all_to_all x1, blocking collectives, on_device(): lax.all_to_all(partial, 'col', split_axis=0, concat_axis=0, tiled=True)  9.5 us
    gather x1, local copies, waits for them, and re-layouts, outgoing_pages(): jnp.take(pool, idx, axis=0)  6.49 us
    sin x1, other arithmetic, attend(): sine = jnp.sin(angles).reshape(req_count, 1, lanes)  5.16 us
  transfers between devices with their start and end apart: 2, of which 1 were waited for; matrix products, arithmetic and copies ran while one was open for 22% of the time, Pallas kernels for 40%

profile of v2, /device:TPU:0, one launch (start us, length us, event | category | flops | bytes accessed | tf_op | source)
XLA Modules:
  0.0 189.2 jit_solution(15497559827469257664)
XLA Ops:
  0.7 0.7 compare_select_fusion.14
  1.4 1.4 scatter_custom_fusion.1
  2.8 1.4 copy.24
  4.3 10.8 %all_gather.6 = bf16[256,512]{1,0:T(8,128)(2,1)S(1)} all-gather(bf16[32,512]{1,0:T(8,128)(2,1)S(1)} %copy-done.5), channel_id=1, replica_groups=mesh['row'=4,'col'=8] {'col'}, dimensions={0}, use_global_device_ids=true | all-gather | bytes 294912 | tf_op jit(solution)/shard_map/all_gather | solution.py:332
  15.1 1.2 gather_fusion.3
  16.2 1.2 convolution_convert_fusion
  17.4 4.9 %all-to-all-start.1 = ((bf16[4,64,768]{2,1,0:T(8,128)(2,1)}), bf16[4,64,768]{2,1,0:T(8,128)(2,1)S(1)}, u32[]{:S(2)}, u32[]{:S(2)}) async-start(bf16[4,64,768]{2,1,0:T(8,128)(2,1)} %bitcast.6), calls=%async_computation.1 | async-start | bytes 786432 | tf_op jit(solution)/shard_map/all_to_all | solution.py:340
  22.5 0.8 select_reduce_fusion
  23.3 0.1 sub.38
  23.4 0.8 scatter_custom_fusion.2
  24.2 0.1 broadcast_in_dim.110
  24.3 6.5 %gather_fusion.6 = bf16[40,64,512]{2,1,0:T(8,128)(2,1)S(1)} fusion(bf16[256,64,512]{2,1,0:T(8,128)(2,1)} %pool_n_ref.1, s32[1024]{0:T(1024)S(1)} %pad_clamp_fusion.4), kind=kCustom, calls=%fused_computation.6 | custom fusion | bytes 5243040 | tf_op jit(solution)/shard_map/jit(_take)/gather | solution.py:289
  30.8 1.8 broadcast_select_fusion.3
  32.6 1.9 all-to-all-done.1
  34.5 3.7 %all-to-all-start.2 = ((bf16[4,10,64,512]{3,2,1,0:T(8,128)(2,1)}), bf16[4,10,64,512]{3,2,1,0:T(8,128)(2,1)S(1)}, u32[]{:S(2)}, u32[]{:S(2)}) async-start(bf16[4,10,64,512]{3,2,1,0:T(8,128)(2,1)} %broadcast_select_fusion.3), calls=%async_computation.2 | async-start | bytes 5242880 | tf_op jit(solution)/shard_map/all_to_all | solution.py:295
  38.2 0.7 gather_fusion.5
  38.8 0.7 gather_fusion.4
  39.5 0.7 reshape.258.tbl
  40.8 0.6 fusion.13
  42.9 0.7 fusion.26
  43.7 4.5 %compare_select_fusion.7 = f32[512,1]{0,1:T(1,128)S(1)} fusion(f32[]{:T(128)} %bitcast.32, f32[]{:T(128)} %bitcast.33, f32[]{:T(128)} %bitcast.34, f32[]{:T(128)} %bitcast.35, f32[]{:T(128)} %bitcast.36, f32[]{:T(128)} %bitcast.38, f32[]{:T(128)} %bitcast.37), kind=kLoop, calls=%fused_computation.80 | loop fusion | flops 16384 | bytes 2076 | tf_op jit(solution)/shard_map/gather | solution.py:206
  48.2 0.7 fusion.25
  48.9 15.6 %select_select_fusion = f32[512]{0:T(512)S(1)} fusion(pred[512]{0:T(512)(128)(4,1)S(1)} %compare_reduce_fusion, pred[512]{0:T(512)(128)(4,1)S(1)} %compare_reduce_fusion.1, pred[512]{0:T(512)(128)(4,1)S(1)} %compare_reduce_fusion.2, pred[512]{0:T(512)(128)(4,1)S(1)} %compare_reduce_fusion.3, pred[512]{0:T(512)(128)(4,1)S(1)} %compare_reduce_fusion.4, ...), kind=kLoop, calls=%fused_computation.98 | loop fusion | flops 12800 | bytes 16996 | tf_op jit(solution)/shard_map/gather | solution.py:206
  64.5 5.2 %multiply_sine_fusion = (f32[64,1,512]{2,1,0:T(1,128)}, f32[64,1,512]{2,1,0:T(1,128)}) fusion(f32[512]{0:T(512)S(1)} %select_select_fusion, f32[64]{0:T(128)S(1)} %convert_element_type.36), kind=kLoop, calls=%fused_computation.37 | loop fusion | flops 32768 | bytes 264448 | tf_op jit(solution)/shard_map/sin | solution.py:208
  69.7 0.7 reshape.261.x_ref
  70.5 76.1 %shard_map.104 = (f32[64,8,128]{2,1,0:T(8,128)}, f32[64,8,128]{2,1,0:T(8,128)}, f32[64,8,512]{2,1,0:T(8,128)}, f32[64,1,512]{2,1,0:T(1,128)}, f32[64,8,128]{2,1,0:T(8,128)}) custom-call(s32[4096]{0:T(1024)} %reshape.258.tbl, s32[64]{0:T(128)} %lens.3, f32[64,1,512]{2,1,0:T(1,128)} %reshape.261.x_ref, f32[64,1,512]{2,1,0:T(1,128)} %get-tuple-element.71.cos_ref, ...), custom_call_target="tpu_custom_call" | custom-call | tf_op jit(solution)/shard_map/pallas_call | solution.py:230
  146.6 3.0 %conditional.1 = (bf16[16,64,512]{2,1,0:T(8,128)(2,1)S(1)}) conditional(s32[]{:T(128)} %clamp.7, (s32[16]{0:T(128)S(1)}, s32[16]{0:T(128)S(1)}, bf16[4,10,64,512]{3,2,1,0:T(8,128)(2,1)S(1)}) %tuple.15, (s32[16]{0:T(128)S(1)}, s32[16]{0:T(128)S(1)}, s32[64]{0:T(128)S(1)}, s32[64]{0:T(128)S(1)}, s32[64]{0:T(128)S(1)}, /*index=5*/s32[64]{0:T(128)S(1)}, ...), branch_computations={%region_7.8_spmd, %region_8.10_spmd} | conditional | flops 3411051 | bytes 23603280 | solution.py:323
  146.7 1.6 gather_fusion
  148.3 1.4 broadcast_select_fusion
  149.7 10.8 %shard_map.105 = (f32[64,8,128]{2,1,0:T(8,128)}, f32[64,8,128]{2,1,0:T(8,128)}, f32[64,8,512]{2,1,0:T(8,128)}) custom-call(s32[4096]{0:T(1024)} %reshape.258.tbl, s32[64]{0:T(128)} %lens.3, f32[64,1,512]{2,1,0:T(1,128)} %get-tuple-element.47.qrow_ref, f32[64,8,128]{2,1,0:T(8,128)} %get-tuple-element.48.m_in, f32[64,8,128]{2,1,0:T(8,128)} %get-tuple-element.49.l_in, ...), custom_call_target="tpu_custom_call" | custom-call | tf_op jit(solution)/shard_map/pallas_call | solution.py:246
  160.5 1.4 slice.40
  161.9 0.8 reshape.262
  162.7 0.1 fusion.24
  162.9 0.1 copy.29
  162.9 0.1 stack.6
  163.2 0.1 copy.32
  163.3 0.1 copy.33
  163.4 0.1 div.52
  163.5 0.1 div.53
  163.6 0.1 copy.30
  163.7 0.1 copy.31
  163.8 0.1 mul.74
  164.0 0.1 mul.75
  164.2 13.4 %all_gather.7 = bf16[256,256]{1,0:T(8,128)(2,1)S(1)} all-gather(bf16[64,256]{1,0:T(8,128)(2,1)S(1)} %divide_convert_fusion), channel_id=1, replica_groups=mesh['row'=4,'col'=8] {'row'}, dimensions={0}, use_global_device_ids=true | all-gather | bytes 163840 | tf_op jit(solution)/shard_map/all_gather | solution.py:348
  177.6 1.2 gather_fusion.7
  178.7 0.3 convolution_convert_fusion.1
  179.0 9.5 %all_to_all.27 = bf16[8,32,512]{2,1,0:T(8,128)(2,1)S(1)} all-to-all(bf16[8,32,512]{2,1,0:T(8,128)(2,1)S(1)} %bitcast.63), channel_id=1, replica_groups=mesh['row'=4,'col'=8] {'col'}, dimensions={0} | all-to-all | bytes 524288 | tf_op jit(solution)/shard_map/all_to_all | solution.py:354
  188.5 0.7 reduce_sum.46
  (75 shorter events, 1.4 us)
Async XLA Ops:
  0.6 178.1 %copy-start = (bf16[256,512]{1,0:T(8,128)(2,1)S(1)}, bf16[256,512]{1,0:T(8,128)(2,1)}, u32[]{:S(2)}) copy-start(bf16[256,512]{1,0:T(8,128)(2,1)} %param.13) | copy-start | bytes 786436
  0.6 3.7 %copy-start.5 = (bf16[32,512]{1,0:T(8,128)(2,1)S(1)}, bf16[32,512]{1,0:T(8,128)(2,1)}, u32[]{:S(2)}) copy-start(bf16[32,512]{1,0:T(8,128)(2,1)} %param.11) | copy-start | bytes 98308
  15.1 7.2 %copy-start.9 = (s32[64]{0:T(128)S(1)}, s32[64]{0:T(128)}, u32[]{:S(2)}) copy-start(s32[64]{0:T(128)} %param.17) | copy-start | bytes 772
  17.4 17.1 %all-to-all-start.1 = ((bf16[4,64,768]{2,1,0:T(8,128)(2,1)}), bf16[4,64,768]{2,1,0:T(8,128)(2,1)S(1)}, u32[]{:S(2)}, u32[]{:S(2)}) async-start(bf16[4,64,768]{2,1,0:T(8,128)(2,1)} %bitcast.6), calls=%async_computation.1 | async-start | bytes 786432 | tf_op jit(solution)/shard_map/all_to_all | solution.py:340
  32.6 6.9 %copy-start.7 = (s32[64]{0:T(128)S(1)}, s32[64]{0:T(128)}, u32[]{:S(2)}) copy-start(s32[64]{0:T(128)} %lens.3) | copy-start | bytes 772
  32.6 6.9 %copy-start.6 = (s32[64,64]{1,0:T(8,128)S(1)}, s32[64,64]{1,0:T(8,128)}, u32[]{:S(2)}) copy-start(s32[64,64]{1,0:T(8,128)} %param.15) | copy-start | bytes 49156
  32.6 16.3 %copy-start.8 = (s32[256]{0:T(256)S(1)}, s32[256]{0:T(256)}, u32[]{:S(2)}) copy-start(s32[256]{0:T(256)} %param.18) | copy-start | bytes 3076
  34.5 112.2 %all-to-all-start.2 = ((bf16[4,10,64,512]{3,2,1,0:T(8,128)(2,1)}), bf16[4,10,64,512]{3,2,1,0:T(8,128)(2,1)S(1)}, u32[]{:S(2)}, u32[]{:S(2)}) async-start(bf16[4,10,64,512]{3,2,1,0:T(8,128)(2,1)} %broadcast_select_fusion.3), calls=%async_computation.2 | async-start | bytes 5242880 | tf_op jit(solution)/shard_map/all_to_all | solution.py:295
  149.7 10.8 %copy-start.1 = (bf16[16,64,512]{2,1,0:T(8,128)(2,1)}, bf16[16,64,512]{2,1,0:T(8,128)(2,1)S(1)}, u32[]{:S(2)}) copy-start(bf16[16,64,512]{2,1,0:T(8,128)(2,1)S(1)} %get-tuple-element.104.land_ref) | copy-start | bytes 3145732
  160.5 2.6 %copy-start.2 = (f32[64,8,128]{2,1,0:T(8,128)S(1)}, f32[64,8,128]{2,1,0:T(8,128)}, u32[]{:S(2)}) copy-start(f32[64,8,128]{2,1,0:T(8,128)} %get-tuple-element.53) | copy-start | bytes 786436
  160.5 2.6 %copy-start.3 = (f32[64,8,128]{2,1,0:T(8,128)S(1)}, f32[64,8,128]{2,1,0:T(8,128)}, u32[]{:S(2)}) copy-start(f32[64,8,128]{2,1,0:T(8,128)} %get-tuple-element.54) | copy-start | bytes 786436
  160.5 2.6 %copy-start.4 = (f32[64,8,128]{2,1,0:T(8,128)S(1)}, f32[64,8,128]{2,1,0:T(8,128)}, u32[]{:S(2)}) copy-start(f32[64,8,128]{2,1,0:T(8,128)} %get-tuple-element.55) | copy-start | bytes 786436

commit v3 on v2

--- a/solution.py
+++ b/solution.py
@@ -203,9 +203,9 @@
     lane = jnp.arange(lanes, dtype=jnp.int32)
     half = HEAD_DIM // 2
     freqs = theta_base ** (-(jnp.arange(half, dtype=jnp.float32) * 2.0 / HEAD_DIM))
-    angles = lens.astype(jnp.float32)[:, None] * freqs[lane % HEAD_DIM % half][None, :]
-    cosine = jnp.cos(angles).reshape(req_count, 1, lanes)
-    sine = jnp.sin(angles).reshape(req_count, 1, lanes)
+    angles = lens.astype(jnp.float32)[:, None] * freqs[None, :]
+    cosine = jnp.tile(jnp.cos(angles), (1, lanes // half)).reshape(req_count, 1, lanes)
+    sine = jnp.tile(jnp.sin(angles), (1, lanes // half)).reshape(req_count, 1, lanes)
     xqk = xqk.reshape(req_count, 1, lanes)
     vf = value_new.astype(jnp.float32).reshape(req_count, heads_here, HEAD_DIM)
     tbl = table.reshape(-1)

time: 190 us -> 163 us (0.86)
  other arithmetic: 32.4 us -> 8.39 us
  Pallas kernels: 86.9 us -> 65.6 us
  blocking collectives: 33.7 us -> 49.9 us
    gather x27 -> x0, other arithmetic: 20.9 us -> none  [attend(): freqs[lane % HEAD_DIM % half][None, :]]
    pallas_call x1, Pallas kernels: 76.1 us -> 59.2 us  [attend(): pl.pallas_call(pool_kernel, grid_spec=pltpu.PrefetchScalarGridSpec(num_sc...]
    all_gather x1, blocking collectives: 13.4 us -> 29.6 us  [on_device(): mixed_all = lax.all_gather(mixed, 'row', axis=0, tiled=True)]
    sin x1, other arithmetic: 5.16 us -> 0.75 us  [attend(): jnp.sin(angles)]
    pallas_call x1, Pallas kernels: 10.8 us -> 6.41 us  [attend(): pl.pallas_call(land_kernel, grid_spec=pltpu.PrefetchScalarGridSpec(num_sc...]
    another operation x0 -> x4, local copies, waits for them, and re-layouts: none -> 2.3 us  [the longest x2 1.5 us: attend(): jnp.tile(jnp.sin(angles), (1, lanes // half)).reshape(req_count, 1, lanes)]
  transfers between devices with their start and end apart: 2 -> 2, of which waited for: 1 -> 1; matrix products, arithmetic and copies ran while one was open for 22% -> 12% of each run, Pallas kernels for 40% -> 37%
where the time goes in v3:
time: 163 us; the launch traced here: 162 us
  Pallas kernels  65.6 us (40%)
  blocking collectives  49.9 us (31%)
  local copies, waits for them, and re-layouts  23.6 us (14%)
  starting transfers between devices  8.52 us (5%)
  other arithmetic  8.39 us (5%)
  between operations  2.16 us (1%)
  waiting for transfers between devices  1.93 us (1%)
    pallas_call x1, Pallas kernels, attend(): pl.pallas_call(pool_kernel, grid_spec=pltpu.PrefetchScalarGridSpec(num_sc...  59.2 us
    all_gather x1, blocking collectives, on_device(): mixed_all = lax.all_gather(mixed, 'row', axis=0, tiled=True)  29.6 us
    all_gather x1, blocking collectives, on_device(): gathered = lax.all_gather(xn, 'col', axis=0, tiled=True)  10.8 us
    all_to_all x1, blocking collectives, on_device(): lax.all_to_all(partial, 'col', split_axis=0, concat_axis=0, tiled=True)  9.5 us
    gather x1, local copies, waits for them, and re-layouts, outgoing_pages(): jnp.take(pool, idx, axis=0)  6.49 us
    pallas_call x1, Pallas kernels, attend(): pl.pallas_call(land_kernel, grid_spec=pltpu.PrefetchScalarGridSpec(num_sc...  6.41 us
    all_to_all x1, starting transfers between devices, on_device(): lax.all_to_all(partial, 'row', split_axis=0, concat_axis=0, tiled=True)  4.87 us
    all_to_all x1, starting transfers between devices, migrate_first(): return lax.all_to_all(sent, 'row', split_axis=0, concat_axis=0, tiled=True)  3.65 us
  transfers between devices with their start and end apart: 2, of which 1 were waited for; matrix products, arithmetic and copies ran while one was open for 12% of the time, Pallas kernels for 37%

profile of v3, /device:TPU:0, one launch (start us, length us, event | category | flops | bytes accessed | tf_op | source)
XLA Modules:
  0.0 161.6 jit_solution(8309540199441506102)
XLA Ops:
  0.7 0.7 compare_select_fusion.5
  1.4 1.4 scatter_custom_fusion.1
  2.8 1.4 copy.26
  4.3 10.8 %all_gather.6 = bf16[256,512]{1,0:T(8,128)(2,1)S(1)} all-gather(bf16[32,512]{1,0:T(8,128)(2,1)S(1)} %copy-done.5), channel_id=1, replica_groups=mesh['row'=4,'col'=8] {'col'}, dimensions={0}, use_global_device_ids=true | all-gather | bytes 294912 | tf_op jit(solution)/shard_map/all_gather | solution.py:332
  15.1 1.2 gather_fusion.3
  16.3 1.2 convolution_convert_fusion
  17.4 4.9 %all-to-all-start.1 = ((bf16[4,64,768]{2,1,0:T(8,128)(2,1)}), bf16[4,64,768]{2,1,0:T(8,128)(2,1)S(1)}, u32[]{:S(2)}, u32[]{:S(2)}) async-start(bf16[4,64,768]{2,1,0:T(8,128)(2,1)} %bitcast.6), calls=%async_computation.1 | async-start | bytes 786432 | tf_op jit(solution)/shard_map/all_to_all | solution.py:340
  22.5 0.7 select_reduce_fusion
  23.3 0.1 sub.38
  23.4 0.8 scatter_custom_fusion.2
  24.3 6.5 %gather_fusion.6 = bf16[40,64,512]{2,1,0:T(8,128)(2,1)S(1)} fusion(bf16[256,64,512]{2,1,0:T(8,128)(2,1)} %pool_n_ref.1, s32[1024]{0:T(1024)S(1)} %pad_clamp_fusion.4), kind=kCustom, calls=%fused_computation.6 | custom fusion | bytes 5243040 | tf_op jit(solution)/shard_map/jit(_take)/gather | solution.py:289
  30.8 1.8 %broadcast_select_fusion.3 = bf16[4,10,64,512]{3,2,1,0:T(8,128)(2,1)} fusion(bf16[4,10,64,512]{3,2,1,0:T(8,128)(2,1)S(1)} %bitcast.27, pred[4,10]{1,0:T(4,128)(4,1)S(1)} %broadcast_in_dim.109), kind=kLoop, calls=%fused_computation.28 | loop fusion | flops 1310720 | bytes 5242920 | tf_op jit(solution)/shard_map/jit(_take)/select_n | solution.py:289
  32.6 1.9 %all-to-all-done.1 = bf16[4,64,768]{2,1,0:T(8,128)(2,1)S(1)} async-done(((bf16[4,64,768]{2,1,0:T(8,128)(2,1)}), bf16[4,64,768]{2,1,0:T(8,128)(2,1)S(1)}, u32[]{:S(2)}, u32[]{:S(2)}) %all-to-all-start.1) | async-done | bytes 393248 | tf_op jit(solution)/shard_map/all_to_all | solution.py:340
  34.5 3.7 %all-to-all-start.2 = ((bf16[4,10,64,512]{3,2,1,0:T(8,128)(2,1)}), bf16[4,10,64,512]{3,2,1,0:T(8,128)(2,1)S(1)}, u32[]{:S(2)}, u32[]{:S(2)}) async-start(bf16[4,10,64,512]{3,2,1,0:T(8,128)(2,1)} %broadcast_select_fusion.3), calls=%async_computation.2 | async-start | bytes 5242880 | tf_op jit(solution)/shard_map/all_to_all | solution.py:295
  38.2 0.7 gather_fusion.5
  38.8 0.7 gather_fusion.4
  39.5 0.8 multiply_sine_fusion
  40.3 0.8 copy.27.cos_ref
  41.1 0.7 tile.18
  41.8 0.8 copy.28.sin_ref
  42.6 1.4 reshape.182.tbl
  44.6 0.6 fusion.12
  45.9 0.6 pad_clamp_fusion.3
  46.5 0.7 compare_and_fusion.5
  47.3 0.7 reshape.185.x_ref
  48.0 59.2 %shard_map.104 = (f32[64,8,128]{2,1,0:T(8,128)}, f32[64,8,128]{2,1,0:T(8,128)}, f32[64,8,512]{2,1,0:T(8,128)}, f32[64,1,512]{2,1,0:T(1,128)}, f32[64,8,128]{2,1,0:T(8,128)}) custom-call(s32[4096]{0:T(1024)} %reshape.182.tbl, s32[64]{0:T(128)} %lens.3, f32[64,1,512]{2,1,0:T(1,128)} %reshape.185.x_ref, f32[64,1,512]{2,1,0:T(1,128)} %copy.27.cos_ref, ...), custom_call_target="tpu_custom_call" | custom-call | tf_op jit(solution)/shard_map/pallas_call | solution.py:230
  107.2 3.0 %conditional.1 = (bf16[16,64,512]{2,1,0:T(8,128)(2,1)S(1)}) conditional(s32[]{:T(128)} %clamp.7, (s32[16]{0:T(128)S(1)}, s32[16]{0:T(128)S(1)}, bf16[4,10,64,512]{3,2,1,0:T(8,128)(2,1)S(1)}) %tuple.15, (s32[16]{0:T(128)S(1)}, s32[16]{0:T(128)S(1)}, s32[64]{0:T(128)S(1)}, s32[64]{0:T(128)S(1)}, s32[64]{0:T(128)S(1)}, /*index=5*/s32[64]{0:T(128)}, ...), branch_computations={%region_7.8_spmd, %region_8.10_spmd} | conditional | flops 3411051 | bytes 23603788 | solution.py:323
  107.3 1.6 gather_fusion
  108.9 1.4 broadcast_select_fusion
  110.3 6.4 %shard_map.105 = (f32[64,8,128]{2,1,0:T(8,128)}, f32[64,8,128]{2,1,0:T(8,128)}, f32[64,8,512]{2,1,0:T(8,128)}) custom-call(s32[4096]{0:T(1024)} %reshape.182.tbl, s32[64]{0:T(128)} %lens.3, f32[64,1,512]{2,1,0:T(1,128)} %get-tuple-element.47.qrow_ref, f32[64,8,128]{2,1,0:T(8,128)} %get-tuple-element.48.m_in, f32[64,8,128]{2,1,0:T(8,128)} %get-tuple-element.49.l_in, ...), custom_call_target="tpu_custom_call" | custom-call | tf_op jit(solution)/shard_map/pallas_call | solution.py:246
  116.7 1.4 slice.40
  118.1 0.8 reshape.186
  118.9 0.1 fusion.23
  119.1 0.1 copy.32
  119.2 0.1 stack.6
  119.4 0.1 copy.35
  119.5 0.1 copy.36
  119.6 0.1 div.52
  119.7 0.1 div.53
  119.9 0.1 copy.33
  120.0 0.1 copy.34
  120.1 0.1 mul.71
  120.2 0.1 mul.72
  120.4 29.6 %all_gather.7 = bf16[256,256]{1,0:T(8,128)(2,1)S(1)} all-gather(bf16[64,256]{1,0:T(8,128)(2,1)S(1)} %divide_convert_fusion), channel_id=1, replica_groups=mesh['row'=4,'col'=8] {'row'}, dimensions={0}, use_global_device_ids=true | all-gather | bytes 163840 | tf_op jit(solution)/shard_map/all_gather | solution.py:348
  150.0 1.2 gather_fusion.7
  151.1 0.3 convolution_convert_fusion.1
  151.4 9.5 %all_to_all.27 = bf16[8,32,512]{2,1,0:T(8,128)(2,1)S(1)} all-to-all(bf16[8,32,512]{2,1,0:T(8,128)(2,1)S(1)} %bitcast.32), channel_id=1, replica_groups=mesh['row'=4,'col'=8] {'col'}, dimensions={0} | all-to-all | bytes 524288 | tf_op jit(solution)/shard_map/all_to_all | solution.py:354
  160.9 0.7 reduce_sum.46
  (50 shorter events, 0.7 us)
Async XLA Ops:
  0.6 150.5 %copy-start = (bf16[256,512]{1,0:T(8,128)(2,1)S(1)}, bf16[256,512]{1,0:T(8,128)(2,1)}, u32[]{:S(2)}) copy-start(bf16[256,512]{1,0:T(8,128)(2,1)} %param.13) | copy-start | bytes 786436
  0.6 3.7 %copy-start.5 = (bf16[32,512]{1,0:T(8,128)(2,1)S(1)}, bf16[32,512]{1,0:T(8,128)(2,1)}, u32[]{:S(2)}) copy-start(bf16[32,512]{1,0:T(8,128)(2,1)} %param.11) | copy-start | bytes 98308
  1.4 1.4 copy-start.6
  15.1 7.2 %copy-start.8 = (s32[64]{0:T(128)S(1)}, s32[64]{0:T(128)}, u32[]{:S(2)}) copy-start(s32[64]{0:T(128)} %param.17) | copy-start | bytes 772
  17.4 17.1 %all-to-all-start.1 = ((bf16[4,64,768]{2,1,0:T(8,128)(2,1)}), bf16[4,64,768]{2,1,0:T(8,128)(2,1)S(1)}, u32[]{:S(2)}, u32[]{:S(2)}) async-start(bf16[4,64,768]{2,1,0:T(8,128)(2,1)} %bitcast.6), calls=%async_computation.1 | async-start | bytes 786432 | tf_op jit(solution)/shard_map/all_to_all | solution.py:340
  22.3 1.9 %copy-start.9 = (s32[64]{0:T(128)}, s32[64]{0:T(128)S(1)}, u32[]{:S(2)}) copy-start(s32[64]{0:T(128)S(1)} %get-tuple-element.62) | copy-start | bytes 772
  32.6 6.9 %copy-start.7 = (s32[64]{0:T(128)S(1)}, s32[64]{0:T(128)}, u32[]{:S(2)}) copy-start(s32[64]{0:T(128)} %lens.3) | copy-start | bytes 772
  34.5 72.7 %all-to-all-start.2 = ((bf16[4,10,64,512]{3,2,1,0:T(8,128)(2,1)}), bf16[4,10,64,512]{3,2,1,0:T(8,128)(2,1)S(1)}, u32[]{:S(2)}, u32[]{:S(2)}) async-start(bf16[4,10,64,512]{3,2,1,0:T(8,128)(2,1)} %broadcast_select_fusion.3), calls=%async_computation.2 | async-start | bytes 5242880 | tf_op jit(solution)/shard_map/all_to_all | solution.py:295
  110.3 6.4 %copy-start.1 = (bf16[16,64,512]{2,1,0:T(8,128)(2,1)}, bf16[16,64,512]{2,1,0:T(8,128)(2,1)S(1)}, u32[]{:S(2)}) copy-start(bf16[16,64,512]{2,1,0:T(8,128)(2,1)S(1)} %get-tuple-element.72.land_ref) | copy-start | bytes 3145732
  116.7 2.6 %copy-start.2 = (f32[64,8,128]{2,1,0:T(8,128)S(1)}, f32[64,8,128]{2,1,0:T(8,128)}, u32[]{:S(2)}) copy-start(f32[64,8,128]{2,1,0:T(8,128)} %get-tuple-element.53) | copy-start | bytes 786436
  116.7 2.6 %copy-start.3 = (f32[64,8,128]{2,1,0:T(8,128)S(1)}, f32[64,8,128]{2,1,0:T(8,128)}, u32[]{:S(2)}) copy-start(f32[64,8,128]{2,1,0:T(8,128)} %get-tuple-element.54) | copy-start | bytes 786436
  116.7 2.6 %copy-start.4 = (f32[64,8,128]{2,1,0:T(8,128)S(1)}, f32[64,8,128]{2,1,0:T(8,128)}, u32[]{:S(2)}) copy-start(f32[64,8,128]{2,1,0:T(8,128)} %get-tuple-element.55) | copy-start | bytes 786436
